TPU v7x, 128 devices: a whole 4x4x4 slice. The times are simulated.
128 devices in a mesh: chan: 8 (over y_hi, x), tm: 16 (over z, y_lo, core).
Axes of the slice: x: 4, y: 4 (y_hi: 2, y_lo: 2; y = y_hi * 2 + y_lo), z: 4, core: 2. Of those that a mesh axis runs over, the one named last changes fastest.
Arguments:
- traces: bfloat16 [128, 1024, 2048], P('tm', 'chan'), may hold values from -6 to 6
- live: int32 [1024], P('chan'), may hold values 0 or 1
Outputs:
- correlations: bfloat16 [1024, 128, 2048], P(('chan', 'tm'))
Inputs may be any that keep to these rules, and one draw needn't show every extreme that they name: `live`: 1 marks a usable channel, 0 a dead one.
All inputs are finite; a program needn't handle non-finite values. No bound on the sum of `live` on one device may be relied on, other than what follows from the above.
Results may differ from a plain program's by a relative error of at most 0.0076.
Values may be sent and summed in bfloat16 or wider, within the bound.
No kernel may reach another device: no remote copies, remote signals or barrier semaphores. Data moves between devices by JAX's collectives and lax.ppermute only.
A program may use at most 128 MiB of HBM per device.

v0:
```python
import math

import jax
import jax.numpy as jnp
import numpy as np
from jax import lax
from jax.experimental import pallas as pl
from jax.experimental.pallas import tpu as pltpu
from jax.sharding import PartitionSpec as P

SMOOTH = 4


def from_behind(block, axis, distance):
    devices = range(lax.axis_size(axis))
    route = [(i - distance, i) for i in devices if i - distance in devices]
    return lax.ppermute(block, axis, route)


def column_bins(count, group_width):
    index = np.arange(count, dtype=np.int64)
    group = index // (2 * group_width)
    within = index % group_width
    is_imag = index // group_width % 2
    return (group * group_width + within, is_imag)


def forward_table(samples, bins, group_width):
    freq, is_imag = column_bins(2 * bins, group_width)
    moments = np.arange(samples, dtype=np.int64)[:, None]
    phase = (moments * freq[None, :] % samples).astype(np.float32) * np.float32(2.0 * math.pi / samples)
    phase = phase.astype(np.float64)
    table = np.where(is_imag[None, :] == 1, -np.sin(phase), np.cos(phase)).astype(np.float32)
    return jnp.asarray(table.astype(jnp.bfloat16))


def inverse_table(samples, bins, group_width, segments):
    freq, is_imag = column_bins(2 * bins, group_width)
    lag = np.arange(samples, dtype=np.int64) - samples // 2
    phase = np.mod(freq[:, None] * lag[None, :], samples).astype(np.float32) * np.float32(
        2.0 * math.pi / samples
    )
    phase = phase.astype(np.float64)
    weight = np.where(freq == 0, 1.0, 2.0).astype(np.float32) / np.float32(math.sqrt(samples * segments))
    wave = np.where(is_imag[:, None] == 1, -np.sin(phase), np.cos(phase)).astype(np.float32)
    return jnp.asarray((weight[:, None] * wave).astype(np.float32).astype(jnp.bfloat16))


def whiten_cols(spectra, groups):
    bins = spectra.shape[0] // 2
    width = bins // groups
    rest = spectra.shape[1:]
    split = spectra.reshape((groups, 2, width) + rest)
    real_part = split[:, 0].reshape((bins,) + rest)
    imag_part = split[:, 1].reshape((bins,) + rest)
    amplitude = jnp.sqrt(real_part * real_part + imag_part * imag_part)
    padded = jnp.pad(amplitude, [(SMOOTH, SMOOTH)] + [(0, 0)] * len(rest))
    smooth = sum((padded[i : i + bins] for i in range(2 * SMOOTH + 1))) / (2 * SMOOTH + 1)
    water = 0.8 * jnp.mean(amplitude, axis=0, keepdims=True) + 1e-06
    level = jnp.maximum(smooth, water).reshape((groups, 1, width) + rest)
    return (split / level).reshape(spectra.shape)


def cross_kernel(own_ref, rev_ref, next_rev_ref, out_ref):
    block = own_ref.shape[2]
    wide = 2 * block
    row = lax.broadcasted_iota(jnp.int32, (block, block), 0)
    col = lax.broadcasted_iota(jnp.int32, (block, block), 1)
    flip = (row + col == block - 1).astype(jnp.bfloat16)
    for f in range(own_ref.shape[1]):
        own_real = own_ref[0, f]
        own_imag = own_ref[1, f]
        lhs = jnp.concatenate(
            [
                jnp.concatenate([own_real, own_imag], axis=1),
                jnp.concatenate([own_imag, -own_real], axis=1),
            ],
            axis=0,
        )
        rhs = jnp.concatenate(
            [
                jnp.concatenate([next_rev_ref[0, f], next_rev_ref[1, f]], axis=1),
                jnp.concatenate([rev_ref[0, f], rev_ref[1, f]], axis=1),
            ],
            axis=0,
        )
        both = lax.dot_general(
            lhs, rhs, (((1,), (1,)), ((), ())), preferred_element_type=jnp.float32
        )
        for part in range(2):
            rows = both[part * block : (part + 1) * block]
            sheared = pltpu.roll(rows, 1, 1, stride=1, stride_axis=0)[:, block:]
            ordered = jnp.dot(
                sheared.astype(jnp.bfloat16), flip, preferred_element_type=jnp.float32
            )
            out_ref[part, f] = ordered.astype(out_ref.dtype)


def cross(own_t, rev_t, next_rev_t, bins_per_step=8, interpret=False):
    two, width, block, segs = own_t.shape
    spec = pl.BlockSpec((two, bins_per_step, block, segs), lambda i: (0, i, 0, 0))
    return pl.pallas_call(
        cross_kernel,
        grid=(width // bins_per_step,),
        in_specs=[spec, spec, spec],
        out_specs=pl.BlockSpec((two, bins_per_step, block, block), lambda i: (0, i, 0, 0)),
        out_shape=jax.ShapeDtypeStruct((two, width, block, block), jnp.bfloat16),
        interpret=interpret,
    )(own_t, rev_t, next_rev_t)


def body(traces, live):
    seg_dev, block, samples = traces.shape
    bins = samples // 2
    groups = lax.axis_size("tm")
    group_width = bins // groups
    segments = seg_dev * groups
    table = forward_table(samples, bins, group_width)
    inverse = inverse_table(samples, bins, group_width, segments)
    spectra = jnp.einsum("jat,tc->cja", traces, table, preferred_element_type=jnp.float32)
    flags = live.astype(jnp.float32)
    white = (whiten_cols(spectra, groups) * flags).astype(jnp.bfloat16)
    own = lax.all_to_all(white, "tm", split_axis=0, concat_axis=1, tiled=True)
    own_t = jnp.swapaxes(own, 1, 2).reshape(2, group_width, block, segments)
    rev_t = own_t[:, :, ::-1, :]
    next_rev_t = from_behind(rev_t, "chan", -1)
    stack = cross(own_t, rev_t, next_rev_t).reshape(2 * group_width, block, block)
    gathered = lax.all_to_all(stack, "tm", split_axis=1, concat_axis=0, tiled=True)
    lagged = jnp.einsum("hak,hl->akl", gathered, inverse, preferred_element_type=jnp.float32)
    return lagged.astype(jnp.bfloat16)


def solution(mesh):
    in_specs = (P("tm", "chan", None), P("chan"))
    out_specs = P(("chan", "tm"), None, None)
    return jax.shard_map(body, mesh=mesh, in_specs=in_specs, out_specs=out_specs, check_vma=False)
```

profile of v0, /device:TPU:6, one launch (start us, length us, event | category | flops | bytes accessed | tf_op | source)
XLA Modules:
  0.0 357.4 jit_solution(14175996468437242201)
XLA Ops:
  0.0 12.5 %fusion.13 = f32[2048,8,128]{2,0,1:T(8,128)S(1)} fusion(bf16[2048,2048,1]{0,1,2:T(8,128)(2,1)} %constant.26, bf16[8,128,2048]{2,1,0:T(8,128)(2,1)} %param.4), kind=kOutput, calls=%fused_computation.19 | convolution fusion | flops 8589934592 | bytes 20971520 | tf_op jit(solution)/shard_map/jat,tc->cja/dot_general | solution.py:120
  12.6 0.0 copy-start
  12.6 3.5 fusion.11
  16.1 0.0 copy-done
  16.1 17.3 %multiply_maximum_fusion = f32[1024,8,128]{2,0,1:T(8,128)S(1)} fusion(f32[1024,8,128]{2,0,1:T(8,128)} %bitcast.31, f32[8,128]{1,0:T(8,128)S(1)} %multiply_add_fusion), kind=kLoop, calls=%fused_computation.10 | loop fusion | flops 10485760 | bytes 8392704 | tf_op jit(solution)/shard_map/max | solution.py:60
  33.4 1.1 fusion.1
  34.4 12.1 %copy.14 = bf16[2048,8,128]{2,1,0:T(8,128)(2,1)S(1)} copy(bf16[2048,8,128]{2,0,1:T(8,128)(2,1)S(1)} %fusion.1) | data formatting | bytes 8388608 | tf_op jit(solution)/shard_map/convert_element_type | solution.py:122
  46.5 56.4 %all_to_all.36 = bf16[2048,8,128]{2,1,0:T(8,128)(2,1)S(1)} all-to-all(bf16[2048,8,128]{2,1,0:T(8,128)(2,1)S(1)} %copy.14), channel_id=1, replica_groups=mesh['chan'=8,'tm'=16] {'tm'}, dimensions={0} | all-to-all | bytes 8388608 | tf_op jit(solution)/shard_map/all_to_all | solution.py:123
  102.9 3.2 copy.25
  106.1 6.4 %copy.16 = bf16[128,128,128]{2,1,0:T(8,128)(2,1)} copy(bf16[128,128,128]{1,2,0:T(8,128)(2,1)} %bitcast.30) | data formatting | bytes 8388608 | tf_op jit(solution)/shard_map/transpose | solution.py:124
  112.5 59.8 %rev.3.rev_ref = bf16[2,64,128,128]{3,2,1,0:T(8,128)(2,1)} reverse(bf16[2,64,128,128]{3,2,1,0:T(8,128)(2,1)} %bitcast.25), dimensions={2} | reverse | bytes 8388608 | tf_op jit(solution)/shard_map/rev | solution.py:125
  172.3 2.7 collective-permute-start
  175.1 94.8 %collective-permute-done.next_rev_ref = bf16[2,64,128,128]{3,2,1,0:T(8,128)(2,1)} collective-permute-done((bf16[2,64,128,128]{3,2,1,0:T(8,128)(2,1)}, bf16[2,64,128,128]{3,2,1,0:T(8,128)(2,1)}, u32[]{:S(2)}, u32[]{:S(2)}) %collective-permute-start) | collective-permute-done | bytes 4194336 | tf_op jit(solution)/shard_map/ppermute | solution.py:17
  269.9 15.1 %shard_map.46 = bf16[2,64,128,128]{3,2,1,0:T(8,128)(2,1)} custom-call(bf16[2,64,128,128]{3,2,1,0:T(8,128)(2,1)} %bitcast.26, bf16[2,64,128,128]{3,2,1,0:T(8,128)(2,1)} %rev.3.rev_ref, bf16[2,64,128,128]{3,2,1,0:T(8,128)(2,1)} %collective-permute-done.next_rev_ref), custom_call_target="tpu_custom_call" | custom-call | tf_op jit(solution)/shard_map/pallas_call | solution.py:102
  285.0 4.9 %copy.17 = bf16[128,128,128]{2,0,1:T(8,128)(2,1)S(1)} copy(bf16[128,128,128]{2,1,0:T(8,128)(2,1)} %bitcast.32) | data formatting | bytes 8388608 | tf_op jit(solution)/shard_map/reshape | solution.py:127
  289.9 0.0 slice-start
  289.9 53.6 %all_to_all.37 = bf16[128,128,128]{2,0,1:T(8,128)(2,1)S(1)} all-to-all(bf16[128,128,128]{2,0,1:T(8,128)(2,1)S(1)} %copy.17), channel_id=1, replica_groups=mesh['chan'=8,'tm'=16] {'tm'}, dimensions={1} | all-to-all | bytes 8388608 | tf_op jit(solution)/shard_map/all_to_all | solution.py:128
  343.5 0.0 slice-start.1
  343.5 2.7 copy.18
  346.2 0.0 slice-done
  346.3 0.0 slice-done.1
  346.3 11.1 %fusion.8 = bf16[8,128,2048]{2,1,0:T(8,128)(2,1)} fusion(bf16[2048,2048,1]{1,0,2:T(8,128)(2,1)S(1)} %bitcast.35, bf16[2048,8,128]{2,1,0:T(8,128)(2,1)S(1)} %bitcast.33), kind=kOutput, calls=%fused_computation.16 | convolution fusion | flops 8592031744 | bytes 16777216 | tf_op jit(solution)/shard_map/hak,hl->akl/dot_general | solution.py:129
  (3 shorter events, 0.0 us)
Async XLA Ops:
  12.6 3.5 copy-start
  172.3 97.5 %collective-permute-start = (bf16[2,64,128,128]{3,2,1,0:T(8,128)(2,1)}, bf16[2,64,128,128]{3,2,1,0:T(8,128)(2,1)}, u32[]{:S(2)}, u32[]{:S(2)}) collective-permute-start(bf16[2,64,128,128]{3,2,1,0:T(8,128)(2,1)} %rev.3.rev_ref), channel_id=1, source_target_pairs={{16,0},{32,16},{48,32},{64,48},{80,64},{96,80},{112,96},{17,1},{33... | collective-permute-start | bytes 12582920 | tf_op jit(solution)/shard_map/ppermute | solution.py:17
  289.9 56.4 %slice-start = ((s8[8388608]{0:T(1024)(128)(4,1)}), s8[4194304]{0:T(1024)(128)(4,1)S(1)}, s32[]{:S(2)}) async-start(s8[8388608]{0:T(1024)(128)(4,1)} %bitcast.34), calls=%async_computation.2 | async-start | bytes 8388608
  343.5 2.7 slice-start.1
where the time goes:
time: 365 us; the launch traced here: 357 us
  blocking collectives  110 us (30%)
  waiting for transfers between devices  94.8 us (26%)
  local copies, waits for them, and re-layouts  89.1 us (24%)
  matrix products  23.7 us (6%)
  other arithmetic  21.9 us (6%)
  Pallas kernels  15.1 us (4%)
    ppermute x1, waiting for transfers between devices, from_behind(): return lax.ppermute(block, axis, route)  94.8 us
    rev x1, local copies, waits for them, and re-layouts, body(): rev_t = own_t[:, :, ::-1, :]  59.8 us
    all_to_all x1, blocking collectives, body(): own = lax.all_to_all(white, 'tm', split_axis=0, concat_axis=1, tiled=True)  56.4 us
    all_to_all x1, blocking collectives, body(): lax.all_to_all(stack, 'tm', split_axis=1, concat_axis=0, tiled=True)  53.6 us
    max x1, other arithmetic, whiten_cols(): level = jnp.maximum(smooth, water).reshape((groups, 1, width) + rest)  17.3 us
    pallas_call x1, Pallas kernels, cross(): pl.pallas_call(cross_kernel, grid=(width // bins_per_step,), in_specs=[sp...  15.1 us
    dot_general x1, matrix products, body(): jnp.einsum('jat,tc->cja', traces, table, preferred_element_type=jnp.float32)  12.5 us
    convert_element_type x1, local copies, waits for them, and re-layouts, body(): white = (whiten_cols(spectra, groups) * flags).astype(jnp.bfloat16)  12.1 us
  transfers between devices with their start and end apart: 1, of which 1 were waited for; matrix products, arithmetic and copies ran while one was open for 0% of the time, Pallas kernels for 0%

commit v1 on v0

--- a/solution.py
+++ b/solution.py
@@ -61,29 +61,24 @@
     return (split / level).reshape(spectra.shape)
 
 
-def cross_kernel(own_ref, rev_ref, next_rev_ref, out_ref):
+def cross_kernel(own_ref, next_ref, out_ref):
     block = own_ref.shape[2]
-    wide = 2 * block
     row = lax.broadcasted_iota(jnp.int32, (block, block), 0)
     col = lax.broadcasted_iota(jnp.int32, (block, block), 1)
     flip = (row + col == block - 1).astype(jnp.bfloat16)
+
+    def reverse_rows(x):
+        return jnp.dot(flip, x, preferred_element_type=jnp.float32).astype(jnp.bfloat16)
+
     for f in range(own_ref.shape[1]):
         own_real = own_ref[0, f]
         own_imag = own_ref[1, f]
+        own_both = jnp.concatenate([own_real, own_imag], axis=1)
         lhs = jnp.concatenate(
-            [
-                jnp.concatenate([own_real, own_imag], axis=1),
-                jnp.concatenate([own_imag, -own_real], axis=1),
-            ],
-            axis=0,
+            [own_both, jnp.concatenate([own_imag, -own_real], axis=1)], axis=0
         )
-        rhs = jnp.concatenate(
-            [
-                jnp.concatenate([next_rev_ref[0, f], next_rev_ref[1, f]], axis=1),
-                jnp.concatenate([rev_ref[0, f], rev_ref[1, f]], axis=1),
-            ],
-            axis=0,
-        )
+        next_both = jnp.concatenate([next_ref[0, f], next_ref[1, f]], axis=1)
+        rhs = jnp.concatenate([reverse_rows(next_both), reverse_rows(own_both)], axis=0)
         both = lax.dot_general(
             lhs, rhs, (((1,), (1,)), ((), ())), preferred_element_type=jnp.float32
         )
@@ -96,17 +91,21 @@
             out_ref[part, f] = ordered.astype(out_ref.dtype)
 
 
-def cross(own_t, rev_t, next_rev_t, bins_per_step=8, interpret=False):
+def cross(own_t, next_t, interpret=False):
     two, width, block, segs = own_t.shape
-    spec = pl.BlockSpec((two, bins_per_step, block, segs), lambda i: (0, i, 0, 0))
+    step = min(width, 8)
+    spec = pl.BlockSpec((two, step, block, segs), lambda i: (0, i, 0, 0))
     return pl.pallas_call(
         cross_kernel,
-        grid=(width // bins_per_step,),
-        in_specs=[spec, spec, spec],
-        out_specs=pl.BlockSpec((two, bins_per_step, block, block), lambda i: (0, i, 0, 0)),
+        grid=(width // step,),
+        in_specs=[spec, spec],
+        out_specs=pl.BlockSpec((two, step, block, block), lambda i: (0, i, 0, 0)),
         out_shape=jax.ShapeDtypeStruct((two, width, block, block), jnp.bfloat16),
         interpret=interpret,
-    )(own_t, rev_t, next_rev_t)
+    )(own_t, next_t)
+
+
+CHUNKS = 2
 
 
 def body(traces, live):
@@ -114,19 +113,27 @@
     bins = samples // 2
     groups = lax.axis_size("tm")
     group_width = bins // groups
+    width = group_width // CHUNKS
     segments = seg_dev * groups
     table = forward_table(samples, bins, group_width)
-    inverse = inverse_table(samples, bins, group_width, segments)
+    inverse = inverse_table(samples, bins, group_width, segments).reshape(
+        groups, 2, CHUNKS, width, samples
+    )
     spectra = jnp.einsum("jat,tc->cja", traces, table, preferred_element_type=jnp.float32)
     flags = live.astype(jnp.float32)
     white = (whiten_cols(spectra, groups) * flags).astype(jnp.bfloat16)
-    own = lax.all_to_all(white, "tm", split_axis=0, concat_axis=1, tiled=True)
-    own_t = jnp.swapaxes(own, 1, 2).reshape(2, group_width, block, segments)
-    rev_t = own_t[:, :, ::-1, :]
-    next_rev_t = from_behind(rev_t, "chan", -1)
-    stack = cross(own_t, rev_t, next_rev_t).reshape(2 * group_width, block, block)
-    gathered = lax.all_to_all(stack, "tm", split_axis=1, concat_axis=0, tiled=True)
-    lagged = jnp.einsum("hak,hl->akl", gathered, inverse, preferred_element_type=jnp.float32)
+    white = white.reshape(groups, 2, CHUNKS, width, seg_dev, block)
+    lagged = None
+    for chunk in range(CHUNKS):
+        piece = white[:, :, chunk].reshape(groups * 2 * width, seg_dev, block)
+        own = lax.all_to_all(piece, "tm", split_axis=0, concat_axis=1, tiled=True)
+        own_t = jnp.swapaxes(own, 1, 2).reshape(2, width, block, segments)
+        next_t = from_behind(own_t, "chan", -1)
+        stack = cross(own_t, next_t).reshape(2 * width, block, block)
+        gathered = lax.all_to_all(stack, "tm", split_axis=1, concat_axis=0, tiled=True)
+        rows = inverse[:, :, chunk].reshape(groups * 2 * width, samples)
+        part = jnp.einsum("hak,hl->akl", gathered, rows, preferred_element_type=jnp.float32)
+        lagged = part if lagged is None else lagged + part
     return lagged.astype(jnp.bfloat16)
 
 

time: 365 us -> 318 us (0.87)
  the two profiles are of different devices: /device:TPU:6 before, /device:TPU:20 now
where the time goes in v1:
time: 318 us
  waiting for transfers between devices  170 us (53%)
  local copies, waits for them, and re-layouts  39.7 us (12%)
  Pallas kernels  33.4 us (11%)
  matrix products  27.7 us (9%)
  starting transfers between devices  25.5 us (8%)
  other arithmetic  21.6 us (7%)
    ppermute x2, waiting for transfers between devices, from_behind(): return lax.ppermute(block, axis, route)  109 us
    all_to_all x2, waiting for transfers between devices, body(): own = lax.all_to_all(piece, 'tm', split_axis=0, concat_axis=1, tiled=True)  41.8 us
    pallas_call x2, Pallas kernels, cross(): pl.pallas_call(cross_kernel, grid=(width // step,), in_specs=[spec, spec]...  33.4 us
    all_to_all x2, waiting for transfers between devices, body(): lax.all_to_all(stack, 'tm', split_axis=1, concat_axis=0, tiled=True)  18.9 us
    max x1, other arithmetic, whiten_cols(): level = jnp.maximum(smooth, water).reshape((groups, 1, width) + rest)  17 us
    dot_general x2, matrix products, body(): jnp.einsum('hak,hl->akl', gathered, rows, preferred_element_type=jnp.floa...  15.2 us
    slice x3, local copies, waits for them, and re-layouts, body(): piece = white[:, :, chunk].reshape(groups * 2 * width, seg_dev, block)  13.1 us
    dot_general x1, matrix products, body(): jnp.einsum('jat,tc->cja', traces, table, preferred_element_type=jnp.float32)  12.5 us
  transfers between devices with their start and end apart: 6, of which 5 were waited for; matrix products, arithmetic and copies ran while one was open for 11% of the time, Pallas kernels for 11%

profile of v1, /device:TPU:20, one launch (start us, length us, event | category | flops | bytes accessed | tf_op | source)
XLA Modules:
  0.0 317.8 jit_solution(14143027737483800376)
XLA Ops:
  0.0 12.5 %fusion.12 = f32[2048,8,128]{2,0,1:T(8,128)S(1)} fusion(bf16[2048,2048,1]{0,1,2:T(8,128)(2,1)} %constant.34, bf16[8,128,2048]{2,1,0:T(8,128)(2,1)} %param.4), kind=kOutput, calls=%fused_computation.22 | convolution fusion | flops 8589934592 | bytes 20971520 | tf_op jit(solution)/shard_map/jat,tc->cja/dot_general | solution.py:122
  12.6 3.5 %fusion.9 = (f32[8,128]{1,0:T(8,128)S(1)}, f32[16,1,64,8,128]{4,2,1,0,3:T(8,128)}) fusion(f32[16,2,64,8,128]{4,2,1,0,3:T(8,128)S(1)} %bitcast.41), kind=kLoop, calls=%fused_computation.20 | loop fusion | flops 4193280 | bytes 12587008 | tf_op jit(solution)/shard_map/reduce_sum | solution.py:59
  16.1 17.0 %multiply_maximum_fusion = f32[1024,8,128]{2,0,1:T(8,128)S(1)} fusion(f32[1024,8,128]{2,0,1:T(8,128)} %bitcast.44, f32[8,128]{1,0:T(8,128)S(1)} %multiply_add_fusion), kind=kLoop, calls=%fused_computation.8 | loop fusion | flops 10485760 | bytes 8392704 | tf_op jit(solution)/shard_map/max | solution.py:60
  36.4 4.7 %copy.13 = bf16[16,2,1,32,8,128]{5,4,3,1,0,2:T(8,128)(2,1)} copy(bf16[16,2,1,32,8,128]{5,3,2,1,0,4:T(8,128)(2,1)S(1)} %get-tuple-element.8) | data formatting | bytes 4194304 | tf_op jit(solution)/shard_map/slice | solution.py:128
  41.0 6.3 %all-to-all-start = ((bf16[1024,8,128]{2,1,0:T(8,128)(2,1)}), bf16[1024,8,128]{2,1,0:T(8,128)(2,1)S(1)}, u32[]{:S(2)}, u32[]{:S(2)}) async-start(bf16[1024,8,128]{2,1,0:T(8,128)(2,1)} %bitcast.53), calls=%async_computation | async-start | bytes 4194304 | tf_op jit(solution)/shard_map/all_to_all | solution.py:129
  47.4 6.2 %copy.19 = bf16[16,2,1,32,8,128]{5,4,3,1,0,2:T(8,128)(2,1)} copy(bf16[16,2,1,32,8,128]{5,3,2,1,0,4:T(8,128)(2,1)} %get-tuple-element.7) | data formatting | bytes 4194304 | tf_op jit(solution)/shard_map/slice | solution.py:128
  53.6 21.6 %all-to-all-done = bf16[1024,8,128]{2,1,0:T(8,128)(2,1)S(1)} async-done(((bf16[1024,8,128]{2,1,0:T(8,128)(2,1)}), bf16[1024,8,128]{2,1,0:T(8,128)(2,1)S(1)}, u32[]{:S(2)}, u32[]{:S(2)}) %all-to-all-start) | async-done | bytes 2097184 | tf_op jit(solution)/shard_map/all_to_all | solution.py:129
  75.2 4.4 %all-to-all-start.2 = ((bf16[1024,8,128]{2,1,0:T(8,128)(2,1)}), bf16[1024,8,128]{2,1,0:T(8,128)(2,1)}, u32[]{:S(2)}, u32[]{:S(2)}) async-start(bf16[1024,8,128]{2,1,0:T(8,128)(2,1)} %bitcast.15), calls=%async_computation.2 | async-start | bytes 4194304 | tf_op jit(solution)/shard_map/all_to_all | solution.py:129
  81.5 3.2 %copy.15 = bf16[64,128,128]{2,1,0:T(8,128)(2,1)S(1)} copy(bf16[64,128,128]{1,2,0:T(8,128)(2,1)} %bitcast.54) | data formatting | bytes 4194304 | tf_op jit(solution)/shard_map/transpose | solution.py:130
  87.2 20.2 %all-to-all-done.2 = bf16[1024,8,128]{2,1,0:T(8,128)(2,1)} async-done(((bf16[1024,8,128]{2,1,0:T(8,128)(2,1)}), bf16[1024,8,128]{2,1,0:T(8,128)(2,1)}, u32[]{:S(2)}, u32[]{:S(2)}) %all-to-all-start.2) | async-done | bytes 2097184 | tf_op jit(solution)/shard_map/all_to_all | solution.py:129
  107.5 3.5 %copy.31 = bf16[64,16,8,128]{3,2,1,0:T(8,128)(2,1)} copy(bf16[64,16,8,128]{3,2,0,1:T(8,128)(2,1)} %bitcast.17) | data formatting | bytes 4194304 | tf_op jit(solution)/shard_map/all_to_all | solution.py:129
  111.0 4.1 %copy.21 = bf16[64,128,128]{2,1,0:T(8,128)(2,1)} copy(bf16[64,128,128]{1,2,0:T(8,128)(2,1)} %bitcast.55) | data formatting | bytes 4194304 | tf_op jit(solution)/shard_map/transpose | solution.py:130
  117.5 17.1 %collective-permute-done.next_ref = bf16[2,32,128,128]{3,2,1,0:T(8,128)(2,1)} collective-permute-done((bf16[2,32,128,128]{3,2,1,0:T(8,128)(2,1)S(1)}, bf16[2,32,128,128]{3,2,1,0:T(8,128)(2,1)}, u32[]{:S(2)}, u32[]{:S(2)}) %collective-permute-start) | collective-permute-done | bytes 2097184 | tf_op jit(solution)/shard_map/ppermute | solution.py:17
  134.5 16.7 %shard_map.46 = bf16[2,32,128,128]{3,2,1,0:T(8,128)(2,1)} custom-call(bf16[2,32,128,128]{3,2,1,0:T(8,128)(2,1)} %bitcast.46, bf16[2,32,128,128]{3,2,1,0:T(8,128)(2,1)} %collective-permute-done.next_ref), custom_call_target="tpu_custom_call" | custom-call | tf_op jit(solution)/shard_map/pallas_call | solution.py:98
  151.3 4.3 %copy.16 = bf16[64,128,128]{2,0,1:T(8,128)(2,1)} copy(bf16[64,128,128]{2,1,0:T(8,128)(2,1)} %bitcast.50) | data formatting | bytes 4194304 | tf_op jit(solution)/shard_map/reshape | solution.py:132
  155.5 5.5 %all-to-all-start.1 = ((bf16[64,128,128]{2,0,1:T(8,128)(2,1)}), bf16[64,128,128]{2,0,1:T(8,128)(2,1)S(1)}, u32[]{:S(2)}, u32[]{:S(2)}) async-start(bf16[64,128,128]{2,0,1:T(8,128)(2,1)} %copy.16), calls=%async_computation.1 | async-start | bytes 4194304 | tf_op jit(solution)/shard_map/all_to_all | solution.py:133
  161.0 92.0 %collective-permute-done.1.next_ref = bf16[2,32,128,128]{3,2,1,0:T(8,128)(2,1)} collective-permute-done((bf16[2,32,128,128]{3,2,1,0:T(8,128)(2,1)}, bf16[2,32,128,128]{3,2,1,0:T(8,128)(2,1)}, u32[]{:S(2)}, u32[]{:S(2)}) %collective-permute-start.1) | collective-permute-done | bytes 2097184 | tf_op jit(solution)/shard_map/ppermute | solution.py:17
  253.0 16.7 %shard_map.47 = bf16[2,32,128,128]{3,2,1,0:T(8,128)(2,1)} custom-call(bf16[2,32,128,128]{3,2,1,0:T(8,128)(2,1)} %bitcast.48, bf16[2,32,128,128]{3,2,1,0:T(8,128)(2,1)} %collective-permute-done.1.next_ref), custom_call_target="tpu_custom_call" | custom-call | tf_op jit(solution)/shard_map/pallas_call | solution.py:98
  269.7 4.3 %copy.22 = bf16[64,128,128]{2,0,1:T(8,128)(2,1)} copy(bf16[64,128,128]{2,1,0:T(8,128)(2,1)} %bitcast.51) | data formatting | bytes 4194304 | tf_op jit(solution)/shard_map/reshape | solution.py:132
  274.0 4.4 %all-to-all-start.3 = ((bf16[64,128,128]{2,0,1:T(8,128)(2,1)}), bf16[64,128,128]{2,0,1:T(8,128)(2,1)}, u32[]{:S(2)}, u32[]{:S(2)}) async-start(bf16[64,128,128]{2,0,1:T(8,128)(2,1)} %copy.22), calls=%async_computation.3 | async-start | bytes 4194304 | tf_op jit(solution)/shard_map/all_to_all | solution.py:133
  280.6 6.8 %fusion.7 = f32[8,128,2048]{2,1,0:T(8,128)} fusion(bf16[1024,2048,1]{1,0,2:T(8,128)(2,1)S(1)} %copy-done.3, bf16[1024,8,128]{2,1,0:T(8,128)(2,1)S(1)} %bitcast.56), kind=kOutput, calls=%fused_computation.16 | convolution fusion | flops 4294967296 | bytes 14680064 | tf_op jit(solution)/shard_map/hak,hl->akl/dot_general | solution.py:135
  287.4 18.9 %all-to-all-done.3 = bf16[64,128,128]{2,0,1:T(8,128)(2,1)} async-done(((bf16[64,128,128]{2,0,1:T(8,128)(2,1)}), bf16[64,128,128]{2,0,1:T(8,128)(2,1)}, u32[]{:S(2)}, u32[]{:S(2)}) %all-to-all-start.3) | async-done | bytes 2097184 | tf_op jit(solution)/shard_map/all_to_all | solution.py:133
  306.3 3.1 copy.23
  309.4 8.4 %add_convert_fusion = bf16[8,128,2048]{2,1,0:T(8,128)(2,1)} fusion(f32[8,128,2048]{2,1,0:T(8,128)} %fusion.7, bf16[1024,2048,1]{1,0,2:T(8,128)(2,1)S(1)} %copy-done.1, bf16[1024,8,128]{2,1,0:T(8,128)(2,1)S(1)} %bitcast.49), kind=kOutput, calls=%fused_computation.3 | convolution fusion | flops 4299161600 | bytes 18874368 | tf_op jit(solution)/shard_map/hak,hl->akl/dot_general | solution.py:135
  (17 shorter events, 12.2 us)
Async XLA Ops:
  12.5 3.5 %copy-start.2 = (s32[128]{0:T(128)S(1)}, s32[128]{0:T(128)}, u32[]{:S(2)}) copy-start(s32[128]{0:T(128)} %param.5) | copy-start | bytes 1540
  41.0 34.1 %all-to-all-start = ((bf16[1024,8,128]{2,1,0:T(8,128)(2,1)}), bf16[1024,8,128]{2,1,0:T(8,128)(2,1)S(1)}, u32[]{:S(2)}, u32[]{:S(2)}) async-start(bf16[1024,8,128]{2,1,0:T(8,128)(2,1)} %bitcast.53), calls=%async_computation | async-start | bytes 4194304 | tf_op jit(solution)/shard_map/all_to_all | solution.py:129
  75.2 32.3 %all-to-all-start.2 = ((bf16[1024,8,128]{2,1,0:T(8,128)(2,1)}), bf16[1024,8,128]{2,1,0:T(8,128)(2,1)}, u32[]{:S(2)}, u32[]{:S(2)}) async-start(bf16[1024,8,128]{2,1,0:T(8,128)(2,1)} %bitcast.15), calls=%async_computation.2 | async-start | bytes 4194304 | tf_op jit(solution)/shard_map/all_to_all | solution.py:129
  84.8 30.3 %copy-start = (bf16[64,128,128]{2,1,0:T(8,128)(2,1)}, bf16[64,128,128]{2,1,0:T(8,128)(2,1)S(1)}, u32[]{:S(2)}) copy-start(bf16[64,128,128]{2,1,0:T(8,128)(2,1)S(1)} %copy.15) | copy-start | bytes 6291460
  84.8 49.8 %collective-permute-start = (bf16[2,32,128,128]{3,2,1,0:T(8,128)(2,1)S(1)}, bf16[2,32,128,128]{3,2,1,0:T(8,128)(2,1)}, u32[]{:S(2)}, u32[]{:S(2)}) collective-permute-start(bf16[2,32,128,128]{3,2,1,0:T(8,128)(2,1)S(1)} %bitcast.45), channel_id=1, source_target_pairs={{16,0},{32,16},{48,32},{64,48},{80,64},{96,80},{112,96},{17,1},{33... | collective-permute-start | bytes 6291464 | tf_op jit(solution)/shard_map/ppermute | solution.py:17
  115.0 138.0 %collective-permute-start.1 = (bf16[2,32,128,128]{3,2,1,0:T(8,128)(2,1)}, bf16[2,32,128,128]{3,2,1,0:T(8,128)(2,1)}, u32[]{:S(2)}, u32[]{:S(2)}) collective-permute-start(bf16[2,32,128,128]{3,2,1,0:T(8,128)(2,1)} %bitcast.47), channel_id=1, source_target_pairs={{16,0},{32,16},{48,32},{64,48},{80,64},{96,80},{112,96},{17,1},{33... | collective-permute-start | bytes 6291464 | tf_op jit(solution)/shard_map/ppermute | solution.py:17
  155.5 118.5 %all-to-all-start.1 = ((bf16[64,128,128]{2,0,1:T(8,128)(2,1)}), bf16[64,128,128]{2,0,1:T(8,128)(2,1)S(1)}, u32[]{:S(2)}, u32[]{:S(2)}) async-start(bf16[64,128,128]{2,0,1:T(8,128)(2,1)} %copy.16), calls=%async_computation.1 | async-start | bytes 4194304 | tf_op jit(solution)/shard_map/all_to_all | solution.py:133
  274.0 32.3 %all-to-all-start.3 = ((bf16[64,128,128]{2,0,1:T(8,128)(2,1)}), bf16[64,128,128]{2,0,1:T(8,128)(2,1)}, u32[]{:S(2)}, u32[]{:S(2)}) async-start(bf16[64,128,128]{2,0,1:T(8,128)(2,1)} %copy.22), calls=%async_computation.3 | async-start | bytes 4194304 | tf_op jit(solution)/shard_map/all_to_all | solution.py:133
  278.5 2.2 copy-start.3
  306.3 3.1 copy-start.1

commit v2 on v1

--- a/solution.py
+++ b/solution.py
@@ -106,6 +106,7 @@
 
 
 CHUNKS = 2
+ROW = 4
 
 
 def body(traces, live):
@@ -123,12 +124,19 @@
     flags = live.astype(jnp.float32)
     white = (whiten_cols(spectra, groups) * flags).astype(jnp.bfloat16)
     white = white.reshape(groups, 2, CHUNKS, width, seg_dev, block)
-    lagged = None
+    blocks = lax.axis_size("chan")
+    inner_route = [(i + 1, i) for i in range(blocks - 1) if (i + 1) % ROW != 0]
+    wrap_route = [(i + 1, i) for i in range(blocks - 1) if (i + 1) % ROW == 0]
+    owns = []
     for chunk in range(CHUNKS):
         piece = white[:, :, chunk].reshape(groups * 2 * width, seg_dev, block)
         own = lax.all_to_all(piece, "tm", split_axis=0, concat_axis=1, tiled=True)
-        own_t = jnp.swapaxes(own, 1, 2).reshape(2, width, block, segments)
-        next_t = from_behind(own_t, "chan", -1)
+        owns.append(jnp.swapaxes(own, 1, 2).reshape(2, width, block, segments))
+    lagged = None
+    for chunk in range(CHUNKS):
+        own_t = owns[chunk]
+        gated, _ = lax.optimization_barrier((own_t, owns[-1]))
+        next_t = lax.ppermute(own_t, "chan", inner_route) + lax.ppermute(gated, "chan", wrap_route)
         stack = cross(own_t, next_t).reshape(2 * width, block, block)
         gathered = lax.all_to_all(stack, "tm", split_axis=1, concat_axis=0, tiled=True)
         rows = inverse[:, :, chunk].reshape(groups * 2 * width, samples)

time: 318 us -> 283 us (0.89)
  the two profiles are of different devices: /device:TPU:20 before, /device:TPU:6 now
where the time goes in v2:
time: 283 us; the launch traced here: 281 us
  waiting for transfers between devices  123 us (43%)
  local copies, waits for them, and re-layouts  39.7 us (14%)
  Pallas kernels  33.4 us (12%)
  starting transfers between devices  28.7 us (10%)
  other arithmetic  28.6 us (10%)
  matrix products  27.7 us (10%)
    ppermute x2, waiting for transfers between devices, body(): lax.ppermute(gated, 'chan', wrap_route)  60.9 us
    all_to_all x2, waiting for transfers between devices, body(): own = lax.all_to_all(piece, 'tm', split_axis=0, concat_axis=1, tiled=True)  44.3 us
    pallas_call x2, Pallas kernels, cross(): pl.pallas_call(cross_kernel, grid=(width // step,), in_specs=[spec, spec]...  33.4 us
    all_to_all x2, waiting for transfers between devices, body(): lax.all_to_all(stack, 'tm', split_axis=1, concat_axis=0, tiled=True)  17.9 us
    max x1, other arithmetic, whiten_cols(): level = jnp.maximum(smooth, water).reshape((groups, 1, width) + rest)  17.3 us
    dot_general x2, matrix products, body(): jnp.einsum('hak,hl->akl', gathered, rows, preferred_element_type=jnp.floa...  15.2 us
    slice x3, local copies, waits for them, and re-layouts, body(): piece = white[:, :, chunk].reshape(groups * 2 * width, seg_dev, block)  13.1 us
    dot_general x1, matrix products, body(): jnp.einsum('jat,tc->cja', traces, table, preferred_element_type=jnp.float32)  12.5 us
  transfers between devices with their start and end apart: 8, of which 5 were waited for; matrix products, arithmetic and copies ran while one was open for 13% of the time, Pallas kernels for 12%

profile of v2, /device:TPU:6, one launch (start us, length us, event | category | flops | bytes accessed | tf_op | source)
XLA Modules:
  0.0 281.3 jit_solution(353439976669594944)
XLA Ops:
  0.0 12.5 %fusion.12 = f32[2048,8,128]{2,0,1:T(8,128)S(1)} fusion(bf16[2048,2048,1]{0,1,2:T(8,128)(2,1)} %constant.34, bf16[8,128,2048]{2,1,0:T(8,128)(2,1)} %param.4), kind=kOutput, calls=%fused_computation.22 | convolution fusion | flops 8589934592 | bytes 20971520 | tf_op jit(solution)/shard_map/jat,tc->cja/dot_general | solution.py:123
  12.6 3.5 %fusion.9 = (f32[8,128]{1,0:T(8,128)S(1)}, f32[16,1,64,8,128]{4,2,1,0,3:T(8,128)}) fusion(f32[16,2,64,8,128]{4,2,1,0,3:T(8,128)S(1)} %bitcast.41), kind=kLoop, calls=%fused_computation.20 | loop fusion | flops 4193280 | bytes 12587008 | tf_op jit(solution)/shard_map/reduce_sum | solution.py:59
  16.1 17.3 %multiply_maximum_fusion = f32[1024,8,128]{2,0,1:T(8,128)S(1)} fusion(f32[1024,8,128]{2,0,1:T(8,128)} %bitcast.44, f32[8,128]{1,0:T(8,128)S(1)} %multiply_add_fusion), kind=kLoop, calls=%fused_computation.8 | loop fusion | flops 10485760 | bytes 8392704 | tf_op jit(solution)/shard_map/max | solution.py:60
  36.6 4.7 %copy.16 = bf16[16,2,1,32,8,128]{5,4,3,1,0,2:T(8,128)(2,1)} copy(bf16[16,2,1,32,8,128]{5,3,2,1,0,4:T(8,128)(2,1)S(1)} %get-tuple-element.11) | data formatting | bytes 4194304 | tf_op jit(solution)/shard_map/slice | solution.py:132
  41.3 6.6 %all-to-all-start.1 = ((bf16[1024,8,128]{2,1,0:T(8,128)(2,1)}), bf16[1024,8,128]{2,1,0:T(8,128)(2,1)S(1)}, u32[]{:S(2)}, u32[]{:S(2)}) async-start(bf16[1024,8,128]{2,1,0:T(8,128)(2,1)} %bitcast.56), calls=%async_computation.1 | async-start | bytes 4194304 | tf_op jit(solution)/shard_map/all_to_all | solution.py:133
  47.9 6.2 %copy.13 = bf16[16,2,1,32,8,128]{5,4,3,1,0,2:T(8,128)(2,1)} copy(bf16[16,2,1,32,8,128]{5,3,2,1,0,4:T(8,128)(2,1)} %get-tuple-element.12) | data formatting | bytes 4194304 | tf_op jit(solution)/shard_map/slice | solution.py:132
  54.2 21.6 %all-to-all-done.1 = bf16[1024,8,128]{2,1,0:T(8,128)(2,1)S(1)} async-done(((bf16[1024,8,128]{2,1,0:T(8,128)(2,1)}), bf16[1024,8,128]{2,1,0:T(8,128)(2,1)S(1)}, u32[]{:S(2)}, u32[]{:S(2)}) %all-to-all-start.1) | async-done | bytes 2097184 | tf_op jit(solution)/shard_map/all_to_all | solution.py:133
  75.8 4.4 %all-to-all-start = ((bf16[1024,8,128]{2,1,0:T(8,128)(2,1)}), bf16[1024,8,128]{2,1,0:T(8,128)(2,1)}, u32[]{:S(2)}, u32[]{:S(2)}) async-start(bf16[1024,8,128]{2,1,0:T(8,128)(2,1)} %bitcast.55), calls=%async_computation | async-start | bytes 4194304 | tf_op jit(solution)/shard_map/all_to_all | solution.py:133
  85.3 22.7 %all-to-all-done = bf16[1024,8,128]{2,1,0:T(8,128)(2,1)} async-done(((bf16[1024,8,128]{2,1,0:T(8,128)(2,1)}), bf16[1024,8,128]{2,1,0:T(8,128)(2,1)}, u32[]{:S(2)}, u32[]{:S(2)}) %all-to-all-start) | async-done | bytes 2097184 | tf_op jit(solution)/shard_map/all_to_all | solution.py:133
  108.0 3.5 %copy.32 = bf16[64,16,8,128]{3,2,1,0:T(8,128)(2,1)} copy(bf16[64,16,8,128]{3,2,0,1:T(8,128)(2,1)} %bitcast.8) | data formatting | bytes 4194304 | tf_op jit(solution)/shard_map/all_to_all | solution.py:133
  111.5 4.1 %copy.15 = bf16[64,128,128]{2,1,0:T(8,128)(2,1)} copy(bf16[64,128,128]{1,2,0:T(8,128)(2,1)} %bitcast.58) | data formatting | bytes 4194304 | tf_op jit(solution)/shard_map/transpose | solution.py:134
  120.6 4.3 %collective-permute-start.2 = (bf16[2,32,128,128]{3,2,1,0:T(8,128)(2,1)S(1)}, bf16[2,32,128,128]{3,2,1,0:T(8,128)(2,1)}, u32[]{:S(2)}, u32[]{:S(2)}) collective-permute-start(bf16[2,32,128,128]{3,2,1,0:T(8,128)(2,1)S(1)} %bitcast.46), channel_id=1, source_target_pairs={{16,0},{32,16},{48,32},{80,64},{96,80},{112,96},{17,1},{33,17},{49... | collective-permute-start | bytes 6291464 | tf_op jit(solution)/shard_map/ppermute | solution.py:139
  124.9 44.9 %collective-permute-done.1 = bf16[2,32,128,128]{3,2,1,0:T(8,128)(2,1)S(1)} collective-permute-done((bf16[2,32,128,128]{3,2,1,0:T(8,128)(2,1)}, bf16[2,32,128,128]{3,2,1,0:T(8,128)(2,1)S(1)}, u32[]{:S(2)}, u32[]{:S(2)}) %collective-permute-start.1) | collective-permute-done | bytes 2097184 | tf_op jit(solution)/shard_map/ppermute | solution.py:139
  171.9 16.7 %shard_map.46 = bf16[2,32,128,128]{3,2,1,0:T(8,128)(2,1)} custom-call(bf16[2,32,128,128]{3,2,1,0:T(8,128)(2,1)} %bitcast.50, bf16[2,32,128,128]{3,2,1,0:T(8,128)(2,1)} %add.62.next_ref), custom_call_target="tpu_custom_call" | custom-call | tf_op jit(solution)/shard_map/pallas_call | solution.py:98
  188.6 4.3 %copy.19 = bf16[64,128,128]{2,0,1:T(8,128)(2,1)} copy(bf16[64,128,128]{2,1,0:T(8,128)(2,1)} %bitcast.52) | data formatting | bytes 4194304 | tf_op jit(solution)/shard_map/reshape | solution.py:140
  192.9 4.7 %all-to-all-start.2 = ((bf16[64,128,128]{2,0,1:T(8,128)(2,1)}), bf16[64,128,128]{2,0,1:T(8,128)(2,1)}, u32[]{:S(2)}, u32[]{:S(2)}) async-start(bf16[64,128,128]{2,0,1:T(8,128)(2,1)} %copy.19), calls=%async_computation.2 | async-start | bytes 4194304 | tf_op jit(solution)/shard_map/all_to_all | solution.py:141
  197.5 16.0 %collective-permute-done.3 = bf16[2,32,128,128]{3,2,1,0:T(8,128)(2,1)} collective-permute-done((bf16[2,32,128,128]{3,2,1,0:T(8,128)(2,1)S(1)}, bf16[2,32,128,128]{3,2,1,0:T(8,128)(2,1)}, u32[]{:S(2)}, u32[]{:S(2)}) %collective-permute-start.3) | collective-permute-done | bytes 2097184 | tf_op jit(solution)/shard_map/ppermute | solution.py:139
  213.5 4.7 %add.63.next_ref = bf16[2,32,128,128]{3,2,1,0:T(8,128)(2,1)} add(bf16[2,32,128,128]{3,2,1,0:T(8,128)(2,1)} %collective-permute-done.2, bf16[2,32,128,128]{3,2,1,0:T(8,128)(2,1)} %collective-permute-done.3) | non-fusion elementwise | flops 1048576 | bytes 6291456 | tf_op jit(solution)/shard_map/add | solution.py:139
  218.2 16.7 %shard_map.47 = bf16[2,32,128,128]{3,2,1,0:T(8,128)(2,1)} custom-call(bf16[2,32,128,128]{3,2,1,0:T(8,128)(2,1)} %bitcast.47, bf16[2,32,128,128]{3,2,1,0:T(8,128)(2,1)} %add.63.next_ref), custom_call_target="tpu_custom_call" | custom-call | tf_op jit(solution)/shard_map/pallas_call | solution.py:98
  234.9 4.3 %copy.22 = bf16[64,128,128]{2,0,1:T(8,128)(2,1)} copy(bf16[64,128,128]{2,1,0:T(8,128)(2,1)} %bitcast.53) | data formatting | bytes 4194304 | tf_op jit(solution)/shard_map/reshape | solution.py:140
  239.3 3.7 %all-to-all-start.3 = ((bf16[64,128,128]{2,0,1:T(8,128)(2,1)}), bf16[64,128,128]{2,0,1:T(8,128)(2,1)S(1)}, u32[]{:S(2)}, u32[]{:S(2)}) async-start(bf16[64,128,128]{2,0,1:T(8,128)(2,1)} %copy.22), calls=%async_computation.3 | async-start | bytes 4194304 | tf_op jit(solution)/shard_map/all_to_all | solution.py:141
  246.1 6.8 %fusion.7 = f32[8,128,2048]{2,1,0:T(8,128)} fusion(bf16[1024,2048,1]{1,0,2:T(8,128)(2,1)S(1)} %copy-done.3, bf16[1024,8,128]{2,1,0:T(8,128)(2,1)S(1)} %bitcast.59), kind=kOutput, calls=%fused_computation.15 | convolution fusion | flops 4294967296 | bytes 14680064 | tf_op jit(solution)/shard_map/hak,hl->akl/dot_general | solution.py:143
  252.9 17.9 %all-to-all-done.3 = bf16[64,128,128]{2,0,1:T(8,128)(2,1)S(1)} async-done(((bf16[64,128,128]{2,0,1:T(8,128)(2,1)}), bf16[64,128,128]{2,0,1:T(8,128)(2,1)S(1)}, u32[]{:S(2)}, u32[]{:S(2)}) %all-to-all-start.3) | async-done | bytes 2097184 | tf_op jit(solution)/shard_map/all_to_all | solution.py:141
  273.0 8.4 %add_convert_fusion = bf16[8,128,2048]{2,1,0:T(8,128)(2,1)} fusion(f32[8,128,2048]{2,1,0:T(8,128)} %fusion.7, bf16[1024,2048,1]{1,0,2:T(8,128)(2,1)S(1)} %copy-done.1, bf16[1024,8,128]{2,1,0:T(8,128)(2,1)S(1)} %bitcast.51), kind=kOutput, calls=%fused_computation.3 | convolution fusion | flops 4299161600 | bytes 18874368 | tf_op jit(solution)/shard_map/hak,hl->akl/dot_general | solution.py:143
  (23 shorter events, 20.7 us)
Async XLA Ops:
  12.6 3.5 %copy-start.2 = (s32[128]{0:T(128)S(1)}, s32[128]{0:T(128)}, u32[]{:S(2)}) copy-start(s32[128]{0:T(128)} %param.5) | copy-start | bytes 1540
  41.3 34.4 %all-to-all-start.1 = ((bf16[1024,8,128]{2,1,0:T(8,128)(2,1)}), bf16[1024,8,128]{2,1,0:T(8,128)(2,1)S(1)}, u32[]{:S(2)}, u32[]{:S(2)}) async-start(bf16[1024,8,128]{2,1,0:T(8,128)(2,1)} %bitcast.56), calls=%async_computation.1 | async-start | bytes 4194304 | tf_op jit(solution)/shard_map/all_to_all | solution.py:133
  75.8 32.3 %all-to-all-start = ((bf16[1024,8,128]{2,1,0:T(8,128)(2,1)}), bf16[1024,8,128]{2,1,0:T(8,128)(2,1)}, u32[]{:S(2)}, u32[]{:S(2)}) async-start(bf16[1024,8,128]{2,1,0:T(8,128)(2,1)} %bitcast.55), calls=%async_computation | async-start | bytes 4194304 | tf_op jit(solution)/shard_map/all_to_all | solution.py:133
  85.3 35.2 %copy-start = (bf16[64,128,128]{2,1,0:T(8,128)(2,1)}, bf16[64,128,128]{2,1,0:T(8,128)(2,1)S(1)}, u32[]{:S(2)}) copy-start(bf16[64,128,128]{2,1,0:T(8,128)(2,1)S(1)} %copy.18) | copy-start | bytes 6291460
  115.6 54.2 %collective-permute-start.1 = (bf16[2,32,128,128]{3,2,1,0:T(8,128)(2,1)}, bf16[2,32,128,128]{3,2,1,0:T(8,128)(2,1)S(1)}, u32[]{:S(2)}, u32[]{:S(2)}) collective-permute-start(bf16[2,32,128,128]{3,2,1,0:T(8,128)(2,1)} %bitcast.48), channel_id=1, source_target_pairs={{64,48},{65,49},{66,50},{67,51},{68,52},{69,53},{70,54},{71,55},{7... | collective-permute-start | bytes 6291464 | tf_op jit(solution)/shard_map/ppermute | solution.py:139
  116.9 52.9 %collective-permute-start = (bf16[2,32,128,128]{3,2,1,0:T(8,128)(2,1)}, bf16[2,32,128,128]{3,2,1,0:T(8,128)(2,1)S(1)}, u32[]{:S(2)}, u32[]{:S(2)}) collective-permute-start(bf16[2,32,128,128]{3,2,1,0:T(8,128)(2,1)} %bitcast.49), channel_id=1, source_target_pairs={{16,0},{32,16},{48,32},{80,64},{96,80},{112,96},{17,1},{33,17},{49... | collective-permute-start | bytes 6291464 | tf_op jit(solution)/shard_map/ppermute | solution.py:139
  119.3 94.3 %collective-permute-start.3 = (bf16[2,32,128,128]{3,2,1,0:T(8,128)(2,1)S(1)}, bf16[2,32,128,128]{3,2,1,0:T(8,128)(2,1)}, u32[]{:S(2)}, u32[]{:S(2)}) collective-permute-start(bf16[2,32,128,128]{3,2,1,0:T(8,128)(2,1)S(1)} %bitcast.45), channel_id=1, source_target_pairs={{64,48},{65,49},{66,50},{67,51},{68,52},{69,53},{70,54},{71,55},{7... | collective-permute-start | bytes 6291464 | tf_op jit(solution)/shard_map/ppermute | solution.py:139
  120.6 93.0 %collective-permute-start.2 = (bf16[2,32,128,128]{3,2,1,0:T(8,128)(2,1)S(1)}, bf16[2,32,128,128]{3,2,1,0:T(8,128)(2,1)}, u32[]{:S(2)}, u32[]{:S(2)}) collective-permute-start(bf16[2,32,128,128]{3,2,1,0:T(8,128)(2,1)S(1)} %bitcast.46), channel_id=1, source_target_pairs={{16,0},{32,16},{48,32},{80,64},{96,80},{112,96},{17,1},{33,17},{49... | collective-permute-start | bytes 6291464 | tf_op jit(solution)/shard_map/ppermute | solution.py:139
  192.9 46.4 %all-to-all-start.2 = ((bf16[64,128,128]{2,0,1:T(8,128)(2,1)}), bf16[64,128,128]{2,0,1:T(8,128)(2,1)}, u32[]{:S(2)}, u32[]{:S(2)}) async-start(bf16[64,128,128]{2,0,1:T(8,128)(2,1)} %copy.19), calls=%async_computation.2 | async-start | bytes 4194304 | tf_op jit(solution)/shard_map/all_to_all | solution.py:141
  239.3 31.5 %all-to-all-start.3 = ((bf16[64,128,128]{2,0,1:T(8,128)(2,1)}), bf16[64,128,128]{2,0,1:T(8,128)(2,1)S(1)}, u32[]{:S(2)}, u32[]{:S(2)}) async-start(bf16[64,128,128]{2,0,1:T(8,128)(2,1)} %copy.22), calls=%async_computation.3 | async-start | bytes 4194304 | tf_op jit(solution)/shard_map/all_to_all | solution.py:141
  243.0 3.1 %copy-start.3 = (bf16[1024,2048,1]{1,0,2:T(8,128)(2,1)S(1)}, bf16[1024,2048,1]{1,0,2:T(8,128)(2,1)}, u32[]{:S(2)}) copy-start(bf16[1024,2048,1]{1,0,2:T(8,128)(2,1)} %constant.35) | copy-start | bytes 12582916
  270.8 2.2 copy-start.1

commit v3 on v2

--- a/solution.py
+++ b/solution.py
@@ -135,8 +135,12 @@
     lagged = None
     for chunk in range(CHUNKS):
         own_t = owns[chunk]
-        gated, _ = lax.optimization_barrier((own_t, owns[-1]))
-        next_t = lax.ppermute(own_t, "chan", inner_route) + lax.ppermute(gated, "chan", wrap_route)
+        if chunk == CHUNKS - 1:
+            next_t = from_behind(own_t, "chan", -1)
+        else:
+            gated, _ = lax.optimization_barrier((own_t, owns[-1]))
+            inner = lax.ppermute(own_t, "chan", inner_route)
+            next_t = inner + lax.ppermute(gated, "chan", wrap_route)
         stack = cross(own_t, next_t).reshape(2 * width, block, block)
         gathered = lax.all_to_all(stack, "tm", split_axis=1, concat_axis=0, tiled=True)
         rows = inverse[:, :, chunk].reshape(groups * 2 * width, samples)
@@ -148,4 +152,5 @@
 def solution(mesh):
     in_specs = (P("tm", "chan", None), P("chan"))
     out_specs = P(("chan", "tm"), None, None)
+
     return jax.shard_map(body, mesh=mesh, in_specs=in_specs, out_specs=out_specs, check_vma=False)

time: 283 us -> 277 us (0.979)
  other arithmetic: 28.6 us -> 23.9 us
  starting transfers between devices: 28.7 us -> 25.4 us
    add x2 -> x1, other arithmetic: 6.79 us -> 2.09 us  [body(): next_t = inner + lax.ppermute(gated, 'chan', wrap_route)]
    ppermute x4 -> x3, starting transfers between devices: 9.28 us -> 5.97 us  [the longest x1 2.37 us: body(): inner = lax.ppermute(own_t, 'chan', inner_route)]
    ppermute x4 -> x3, waiting for transfers between devices: 60.9 us -> 64.2 us  [the longest x1 48.2 us: body(): next_t = inner + lax.ppermute(gated, 'chan', wrap_route)]
  transfers between devices with their start and end apart: 8 -> 7, of which waited for: 5 -> 5; matrix products, arithmetic and copies ran while one was open for 13% -> 12% of each run, Pallas kernels for 12% -> 12%
where the time goes in v3:
time: 277 us; the launch traced here: 276 us
  waiting for transfers between devices  125 us (45%)
  local copies, waits for them, and re-layouts  39.7 us (14%)
  Pallas kernels  33.4 us (12%)
  matrix products  27.7 us (10%)
  starting transfers between devices  25.4 us (9%)
  other arithmetic  23.9 us (9%)
    ppermute x1, waiting for transfers between devices, body(): next_t = inner + lax.ppermute(gated, 'chan', wrap_route)  48.2 us
    all_to_all x2, waiting for transfers between devices, body(): own = lax.all_to_all(piece, 'tm', split_axis=0, concat_axis=1, tiled=True)  43.4 us
    pallas_call x2, Pallas kernels, cross(): pl.pallas_call(cross_kernel, grid=(width // step,), in_specs=[spec, spec]...  33.4 us
    all_to_all x2, waiting for transfers between devices, body(): lax.all_to_all(stack, 'tm', split_axis=1, concat_axis=0, tiled=True)  17.9 us
    max x1, other arithmetic, whiten_cols(): level = jnp.maximum(smooth, water).reshape((groups, 1, width) + rest)  17.3 us
    ppermute x1, waiting for transfers between devices, from_behind(): return lax.ppermute(block, axis, route)  16 us
    dot_general x2, matrix products, body(): jnp.einsum('hak,hl->akl', gathered, rows, preferred_element_type=jnp.floa...  15.2 us
    slice x3, local copies, waits for them, and re-layouts, body(): piece = white[:, :, chunk].reshape(groups * 2 * width, seg_dev, block)  13.1 us
  transfers between devices with their start and end apart: 7, of which 5 were waited for; matrix products, arithmetic and copies ran while one was open for 12% of the time, Pallas kernels for 12%

profile of v3, /device:TPU:6, one launch (start us, length us, event | category | flops | bytes accessed | tf_op | source)
XLA Modules:
  0.0 275.8 jit_solution(11641009484042343885)
XLA Ops:
  0.0 12.5 %fusion.12 = f32[2048,8,128]{2,0,1:T(8,128)S(1)} fusion(bf16[2048,2048,1]{0,1,2:T(8,128)(2,1)} %constant.34, bf16[8,128,2048]{2,1,0:T(8,128)(2,1)} %param.4), kind=kOutput, calls=%fused_computation.22 | convolution fusion | flops 8589934592 | bytes 20971520 | tf_op jit(solution)/shard_map/jat,tc->cja/dot_general | solution.py:123
  12.6 3.5 %fusion.9 = (f32[8,128]{1,0:T(8,128)S(1)}, f32[16,1,64,8,128]{4,2,1,0,3:T(8,128)}) fusion(f32[16,2,64,8,128]{4,2,1,0,3:T(8,128)S(1)} %bitcast.41), kind=kLoop, calls=%fused_computation.20 | loop fusion | flops 4193280 | bytes 12587008 | tf_op jit(solution)/shard_map/reduce_sum | solution.py:59
  16.1 17.3 %multiply_maximum_fusion = f32[1024,8,128]{2,0,1:T(8,128)S(1)} fusion(f32[1024,8,128]{2,0,1:T(8,128)} %bitcast.44, f32[8,128]{1,0:T(8,128)S(1)} %multiply_add_fusion), kind=kLoop, calls=%fused_computation.8 | loop fusion | flops 10485760 | bytes 8392704 | tf_op jit(solution)/shard_map/max | solution.py:60
  36.6 4.7 %copy.13 = bf16[16,2,1,32,8,128]{5,4,3,1,0,2:T(8,128)(2,1)} copy(bf16[16,2,1,32,8,128]{5,3,2,1,0,4:T(8,128)(2,1)S(1)} %get-tuple-element.10) | data formatting | bytes 4194304 | tf_op jit(solution)/shard_map/slice | solution.py:132
  41.3 6.6 %all-to-all-start = ((bf16[1024,8,128]{2,1,0:T(8,128)(2,1)}), bf16[1024,8,128]{2,1,0:T(8,128)(2,1)S(1)}, u32[]{:S(2)}, u32[]{:S(2)}) async-start(bf16[1024,8,128]{2,1,0:T(8,128)(2,1)} %bitcast.55), calls=%async_computation | async-start | bytes 4194304 | tf_op jit(solution)/shard_map/all_to_all | solution.py:133
  47.9 6.2 %copy.16 = bf16[16,2,1,32,8,128]{5,4,3,1,0,2:T(8,128)(2,1)} copy(bf16[16,2,1,32,8,128]{5,3,2,1,0,4:T(8,128)(2,1)} %get-tuple-element.9) | data formatting | bytes 4194304 | tf_op jit(solution)/shard_map/slice | solution.py:132
  54.2 21.6 %all-to-all-done = bf16[1024,8,128]{2,1,0:T(8,128)(2,1)S(1)} async-done(((bf16[1024,8,128]{2,1,0:T(8,128)(2,1)}), bf16[1024,8,128]{2,1,0:T(8,128)(2,1)S(1)}, u32[]{:S(2)}, u32[]{:S(2)}) %all-to-all-start) | async-done | bytes 2097184 | tf_op jit(solution)/shard_map/all_to_all | solution.py:133
  75.7 4.4 %all-to-all-start.1 = ((bf16[1024,8,128]{2,1,0:T(8,128)(2,1)}), bf16[1024,8,128]{2,1,0:T(8,128)(2,1)}, u32[]{:S(2)}, u32[]{:S(2)}) async-start(bf16[1024,8,128]{2,1,0:T(8,128)(2,1)} %bitcast.54), calls=%async_computation.1 | async-start | bytes 4194304 | tf_op jit(solution)/shard_map/all_to_all | solution.py:133
  82.1 4.1 %copy.15 = bf16[64,128,128]{2,1,0:T(8,128)(2,1)} copy(bf16[64,128,128]{1,2,0:T(8,128)(2,1)} %bitcast.56) | data formatting | bytes 4194304 | tf_op jit(solution)/shard_map/transpose | solution.py:134
  86.2 21.8 %all-to-all-done.1 = bf16[1024,8,128]{2,1,0:T(8,128)(2,1)} async-done(((bf16[1024,8,128]{2,1,0:T(8,128)(2,1)}), bf16[1024,8,128]{2,1,0:T(8,128)(2,1)}, u32[]{:S(2)}, u32[]{:S(2)}) %all-to-all-start.1) | async-done | bytes 2097184 | tf_op jit(solution)/shard_map/all_to_all | solution.py:133
  108.0 3.5 %copy.31 = bf16[64,16,8,128]{3,2,1,0:T(8,128)(2,1)} copy(bf16[64,16,8,128]{3,2,0,1:T(8,128)(2,1)} %bitcast.14) | data formatting | bytes 4194304 | tf_op jit(solution)/shard_map/all_to_all | solution.py:133
  111.5 3.2 %copy.18 = bf16[64,128,128]{2,1,0:T(8,128)(2,1)S(1)} copy(bf16[64,128,128]{1,2,0:T(8,128)(2,1)} %bitcast.57) | data formatting | bytes 4194304 | tf_op jit(solution)/shard_map/transpose | solution.py:134
  120.7 48.2 %collective-permute-done.1 = bf16[2,32,128,128]{3,2,1,0:T(8,128)(2,1)S(1)} collective-permute-done((bf16[2,32,128,128]{3,2,1,0:T(8,128)(2,1)}, bf16[2,32,128,128]{3,2,1,0:T(8,128)(2,1)S(1)}, u32[]{:S(2)}, u32[]{:S(2)}) %collective-permute-start.1) | collective-permute-done | bytes 2097184 | tf_op jit(solution)/shard_map/ppermute | solution.py:143
  171.1 16.7 %shard_map.46 = bf16[2,32,128,128]{3,2,1,0:T(8,128)(2,1)} custom-call(bf16[2,32,128,128]{3,2,1,0:T(8,128)(2,1)} %bitcast.49, bf16[2,32,128,128]{3,2,1,0:T(8,128)(2,1)} %add.59.next_ref), custom_call_target="tpu_custom_call" | custom-call | tf_op jit(solution)/shard_map/pallas_call | solution.py:98
  187.8 4.3 %copy.19 = bf16[64,128,128]{2,0,1:T(8,128)(2,1)} copy(bf16[64,128,128]{2,1,0:T(8,128)(2,1)} %bitcast.51) | data formatting | bytes 4194304 | tf_op jit(solution)/shard_map/reshape | solution.py:144
  192.0 4.7 %all-to-all-start.2 = ((bf16[64,128,128]{2,0,1:T(8,128)(2,1)}), bf16[64,128,128]{2,0,1:T(8,128)(2,1)}, u32[]{:S(2)}, u32[]{:S(2)}) async-start(bf16[64,128,128]{2,0,1:T(8,128)(2,1)} %copy.19), calls=%async_computation.2 | async-start | bytes 4194304 | tf_op jit(solution)/shard_map/all_to_all | solution.py:145
  196.7 16.0 %collective-permute-done.2.next_ref = bf16[2,32,128,128]{3,2,1,0:T(8,128)(2,1)} collective-permute-done((bf16[2,32,128,128]{3,2,1,0:T(8,128)(2,1)S(1)}, bf16[2,32,128,128]{3,2,1,0:T(8,128)(2,1)}, u32[]{:S(2)}, u32[]{:S(2)}) %collective-permute-start.2) | collective-permute-done | bytes 2097184 | tf_op jit(solution)/shard_map/ppermute | solution.py:17
  212.7 16.7 %shard_map.47 = bf16[2,32,128,128]{3,2,1,0:T(8,128)(2,1)} custom-call(bf16[2,32,128,128]{3,2,1,0:T(8,128)(2,1)} %bitcast.46, bf16[2,32,128,128]{3,2,1,0:T(8,128)(2,1)} %collective-permute-done.2.next_ref), custom_call_target="tpu_custom_call" | custom-call | tf_op jit(solution)/shard_map/pallas_call | solution.py:98
  229.4 4.3 %copy.22 = bf16[64,128,128]{2,0,1:T(8,128)(2,1)} copy(bf16[64,128,128]{2,1,0:T(8,128)(2,1)} %bitcast.52) | data formatting | bytes 4194304 | tf_op jit(solution)/shard_map/reshape | solution.py:144
  233.7 3.7 %all-to-all-start.3 = ((bf16[64,128,128]{2,0,1:T(8,128)(2,1)}), bf16[64,128,128]{2,0,1:T(8,128)(2,1)S(1)}, u32[]{:S(2)}, u32[]{:S(2)}) async-start(bf16[64,128,128]{2,0,1:T(8,128)(2,1)} %copy.22), calls=%async_computation.3 | async-start | bytes 4194304 | tf_op jit(solution)/shard_map/all_to_all | solution.py:145
  237.5 3.1 %copy.20 = bf16[64,128,128]{2,1,0:T(8,128)(2,1)S(1)} copy(bf16[64,128,128]{2,0,1:T(8,128)(2,1)} %all-to-all-done.2) | data formatting | bytes 4194304 | tf_op jit(solution)/shard_map/all_to_all | solution.py:145
  240.6 6.8 %fusion.7 = f32[8,128,2048]{2,1,0:T(8,128)} fusion(bf16[1024,2048,1]{1,0,2:T(8,128)(2,1)S(1)} %copy-done.3, bf16[1024,8,128]{2,1,0:T(8,128)(2,1)S(1)} %bitcast.58), kind=kOutput, calls=%fused_computation.15 | convolution fusion | flops 4294967296 | bytes 14680064 | tf_op jit(solution)/shard_map/hak,hl->akl/dot_general | solution.py:147
  247.4 17.9 %all-to-all-done.3 = bf16[64,128,128]{2,0,1:T(8,128)(2,1)S(1)} async-done(((bf16[64,128,128]{2,0,1:T(8,128)(2,1)}), bf16[64,128,128]{2,0,1:T(8,128)(2,1)S(1)}, u32[]{:S(2)}, u32[]{:S(2)}) %all-to-all-start.3) | async-done | bytes 2097184 | tf_op jit(solution)/shard_map/all_to_all | solution.py:145
  267.4 8.4 %add_convert_fusion = bf16[8,128,2048]{2,1,0:T(8,128)(2,1)} fusion(f32[8,128,2048]{2,1,0:T(8,128)} %fusion.7, bf16[1024,2048,1]{1,0,2:T(8,128)(2,1)S(1)} %copy-done.1, bf16[1024,8,128]{2,1,0:T(8,128)(2,1)S(1)} %bitcast.50), kind=kOutput, calls=%fused_computation.3 | convolution fusion | flops 4299161600 | bytes 18874368 | tf_op jit(solution)/shard_map/hak,hl->akl/dot_general | solution.py:147
  (20 shorter events, 15.5 us)
Async XLA Ops:
  12.6 3.5 %copy-start.2 = (s32[128]{0:T(128)S(1)}, s32[128]{0:T(128)}, u32[]{:S(2)}) copy-start(s32[128]{0:T(128)} %param.5) | copy-start | bytes 1540
  41.3 34.4 %all-to-all-start = ((bf16[1024,8,128]{2,1,0:T(8,128)(2,1)}), bf16[1024,8,128]{2,1,0:T(8,128)(2,1)S(1)}, u32[]{:S(2)}, u32[]{:S(2)}) async-start(bf16[1024,8,128]{2,1,0:T(8,128)(2,1)} %bitcast.55), calls=%async_computation | async-start | bytes 4194304 | tf_op jit(solution)/shard_map/all_to_all | solution.py:133
  75.7 32.3 %all-to-all-start.1 = ((bf16[1024,8,128]{2,1,0:T(8,128)(2,1)}), bf16[1024,8,128]{2,1,0:T(8,128)(2,1)}, u32[]{:S(2)}, u32[]{:S(2)}) async-start(bf16[1024,8,128]{2,1,0:T(8,128)(2,1)} %bitcast.54), calls=%async_computation.1 | async-start | bytes 4194304 | tf_op jit(solution)/shard_map/all_to_all | solution.py:133
  114.7 73.0 %copy-start = (bf16[64,128,128]{2,1,0:T(8,128)(2,1)}, bf16[64,128,128]{2,1,0:T(8,128)(2,1)S(1)}, u32[]{:S(2)}) copy-start(bf16[64,128,128]{2,1,0:T(8,128)(2,1)S(1)} %copy.18) | copy-start | bytes 6291460
  114.7 54.2 %collective-permute-start.1 = (bf16[2,32,128,128]{3,2,1,0:T(8,128)(2,1)}, bf16[2,32,128,128]{3,2,1,0:T(8,128)(2,1)S(1)}, u32[]{:S(2)}, u32[]{:S(2)}) collective-permute-start(bf16[2,32,128,128]{3,2,1,0:T(8,128)(2,1)} %bitcast.47), channel_id=1, source_target_pairs={{64,48},{65,49},{66,50},{67,51},{68,52},{69,53},{70,54},{71,55},{7... | collective-permute-start | bytes 6291464 | tf_op jit(solution)/shard_map/ppermute | solution.py:143
  116.0 52.9 %collective-permute-start = (bf16[2,32,128,128]{3,2,1,0:T(8,128)(2,1)}, bf16[2,32,128,128]{3,2,1,0:T(8,128)(2,1)S(1)}, u32[]{:S(2)}, u32[]{:S(2)}) collective-permute-start(bf16[2,32,128,128]{3,2,1,0:T(8,128)(2,1)} %bitcast.48), channel_id=1, source_target_pairs={{16,0},{32,16},{48,32},{80,64},{96,80},{112,96},{17,1},{33,17},{49... | collective-permute-start | bytes 6291464 | tf_op jit(solution)/shard_map/ppermute | solution.py:142
  118.4 94.3 %collective-permute-start.2 = (bf16[2,32,128,128]{3,2,1,0:T(8,128)(2,1)S(1)}, bf16[2,32,128,128]{3,2,1,0:T(8,128)(2,1)}, u32[]{:S(2)}, u32[]{:S(2)}) collective-permute-start(bf16[2,32,128,128]{3,2,1,0:T(8,128)(2,1)S(1)} %bitcast.45), channel_id=1, source_target_pairs={{16,0},{32,16},{48,32},{64,48},{80,64},{96,80},{112,96},{17,1},{33... | collective-permute-start | bytes 6291464 | tf_op jit(solution)/shard_map/ppermute | solution.py:17
  192.0 41.7 %all-to-all-start.2 = ((bf16[64,128,128]{2,0,1:T(8,128)(2,1)}), bf16[64,128,128]{2,0,1:T(8,128)(2,1)}, u32[]{:S(2)}, u32[]{:S(2)}) async-start(bf16[64,128,128]{2,0,1:T(8,128)(2,1)} %copy.19), calls=%async_computation.2 | async-start | bytes 4194304 | tf_op jit(solution)/shard_map/all_to_all | solution.py:145
  233.7 31.5 %all-to-all-start.3 = ((bf16[64,128,128]{2,0,1:T(8,128)(2,1)}), bf16[64,128,128]{2,0,1:T(8,128)(2,1)S(1)}, u32[]{:S(2)}, u32[]{:S(2)}) async-start(bf16[64,128,128]{2,0,1:T(8,128)(2,1)} %copy.22), calls=%async_computation.3 | async-start | bytes 4194304 | tf_op jit(solution)/shard_map/all_to_all | solution.py:145
  237.5 3.1 %copy-start.3 = (bf16[1024,2048,1]{1,0,2:T(8,128)(2,1)S(1)}, bf16[1024,2048,1]{1,0,2:T(8,128)(2,1)}, u32[]{:S(2)}) copy-start(bf16[1024,2048,1]{1,0,2:T(8,128)(2,1)} %constant.35) | copy-start | bytes 12582916
  265.2 2.2 copy-start.1
